TPU v7x, 32 devices: a whole 2x2x4 slice. The times are simulated.
32 devices in a mesh: section: 2 (over core), dp: 16 (over z, y, x).
Axes of the slice: x: 2, y: 2, z: 4, core: 2. Of those that a mesh axis runs over, the one named last changes fastest.
Arguments:
- acts: bfloat16 [2, 16, 1, 64, 2, 2, 128], P('section', 'dp'), may hold values from -6 to 6
- preacts: bfloat16 [2, 16, 1, 64, 2, 2, 128], P('section', 'dp'), may hold values from -6 to 6
- top_grad: bfloat16 [16, 1, 64, 2, 2, 128], P('dp'), may hold values from -6 to 6
- weights: bfloat16 [2, 64, 1728], P('section'), may hold values from -0.21875 to 0.21875
- a_factor: bfloat16 [2, 1728, 1728], P('section', 'dp'), as said below
- g_factor: bfloat16 [2, 64, 64], P('section'), as said below
Outputs:
- act_grads: bfloat16 [2, 16, 1, 64, 2, 2, 128], P('section', 'dp')
- update: float32 [2, 1728, 64], P('section', 'dp')
- inverse: float32 [2, 1728, 1728], P('section', 'dp')
Inputs may be any that keep to these rules, and one draw needn't show every extreme that they name: `a_factor`: each matrix is symmetric and positive definite. `g_factor`: each matrix is symmetric and positive definite.
All inputs are finite; a program needn't handle non-finite values. Where the computation divides by a largest or mean magnitude, that divisor is 1e-20 or more.
Results may differ from a plain program's by a relative error of at most 0.006.
Values may be sent and summed in bfloat16 or wider, within the bound.
No kernel may reach another device: no remote copies, remote signals or barrier semaphores. Data moves between devices by JAX's collectives and lax.ppermute only.
A program may use at most 64 MiB of HBM per device.

v0:
```python
import jax
import jax.numpy as jnp
from jax import lax
from jax.sharding import PartitionSpec as P

KW = 3
MICRO = 1


def shifted(value, axis, steps):
    count = lax.axis_size(axis)
    first, last = (max(0, -steps), min(count, count - steps))
    return lax.ppermute(value, axis, [(source, source + steps) for source in range(first, last)])


def tap_offsets(kernel_width):
    middle = kernel_width // 2
    result = []
    for along_x in range(kernel_width):
        for along_y in range(kernel_width):
            for along_z in range(kernel_width):
                result.append((along_x - middle, along_y - middle, along_z - middle))
    return result


def taps_stack(volume, kernel_width, direction):
    middle = kernel_width // 2
    padded = jnp.pad(volume, ((0, 0), (middle, middle), (middle, middle), (middle, middle)))
    size_x, size_y, size_z = (volume.shape[1], volume.shape[2], volume.shape[3])
    pieces = []
    for off_x, off_y, off_z in tap_offsets(kernel_width):
        start_x = middle + direction * off_x
        start_y = middle + direction * off_y
        start_z = middle + direction * off_z
        pieces.append(
            padded[
                :,
                start_x : start_x + size_x,
                start_y : start_y + size_y,
                start_z : start_z + size_z,
            ]
        )
    stacked = jnp.stack(pieces, 0)
    return stacked.reshape(len(pieces) * volume.shape[0], size_x * size_y * size_z)


def back_input(grad_out, w_rows):
    columns = taps_stack(grad_out, KW, -1)
    summed = lax.dot_general(
        w_rows, columns, (((0,), (0,)), ((), ())), preferred_element_type=jnp.float32
    )
    return summed.astype(jnp.bfloat16).reshape(grad_out.shape)


def back_weight(volume, grad_out):
    columns = taps_stack(volume, KW, 1)
    flattened = grad_out.reshape(grad_out.shape[0], -1)
    return lax.dot_general(
        columns, flattened, (((1,), (1,)), ((), ())), preferred_element_type=jnp.float32
    )


def local_inverse(matrix):
    values = matrix.astype(jnp.float32)
    step_size = 1.0 / jnp.max(jnp.sum(jnp.abs(values), axis=1))
    identity = jnp.eye(matrix.shape[0], dtype=jnp.float32)
    resid0 = (identity - step_size * values).astype(jnp.bfloat16)
    resid1 = jnp.dot(resid0, resid0, preferred_element_type=jnp.float32).astype(jnp.bfloat16)
    cross_term = jnp.dot(resid1, resid0, preferred_element_type=jnp.float32)
    return step_size * (
        identity + resid0.astype(jnp.float32) + resid1.astype(jnp.float32) + cross_term
    )


def eye_rows(start_row, row_total, order_full):
    column_ids = lax.broadcasted_iota(jnp.int32, (row_total, order_full), 1)
    row_ids = lax.broadcasted_iota(jnp.int32, (row_total, order_full), 0)
    return (column_ids == start_row + row_ids).astype(jnp.float32)


def shards(acts, preacts, top_grad, weights, a_factor, g_factor):
    section_index = lax.axis_index("section")
    section_count = lax.axis_size("section")
    tick_count = MICRO + section_count - 1
    inputs = acts[0, 0]
    pre_values = preacts[0, 0]
    upper_grads = top_grad[0]
    channels = weights.shape[1]
    w_rows = weights[0].reshape(channels, -1, channels).transpose(1, 0, 2).reshape(-1, channels)
    zero_field = jnp.zeros(inputs.shape[1:], jnp.bfloat16)

    def one_tick(tick_index, carried):
        outgoing, stored_grads, stored_slopes = carried
        incoming = shifted(outgoing, "section", -1)
        micro_index = tick_index - (section_count - 1 - section_index)
        is_valid = jnp.logical_and(micro_index >= 0, micro_index < MICRO)
        clipped = jnp.clip(micro_index, 0, MICRO - 1)
        from_top = lax.dynamic_index_in_dim(upper_grads, clipped, 0, keepdims=False)
        arriving = jnp.where(section_index == section_count - 1, from_top, incoming)
        pre_now = lax.dynamic_index_in_dim(pre_values, clipped, 0, keepdims=False)
        grad_out = jnp.where(pre_now > 0, arriving, zero_field)
        sending = back_input(grad_out, w_rows)
        old_grad = lax.dynamic_index_in_dim(stored_grads, clipped, 0, keepdims=False)
        old_slope = lax.dynamic_index_in_dim(stored_slopes, clipped, 0, keepdims=False)
        stored_grads = lax.dynamic_update_index_in_dim(
            stored_grads, jnp.where(is_valid, sending, old_grad), clipped, 0
        )
        stored_slopes = lax.dynamic_update_index_in_dim(
            stored_slopes, jnp.where(is_valid, grad_out, old_slope), clipped, 0
        )
        return (sending, stored_grads, stored_slopes)

    start_state = (
        zero_field,
        jnp.zeros(inputs.shape, jnp.bfloat16),
        jnp.zeros(inputs.shape, jnp.bfloat16),
    )
    last_sent, stored_grads, stored_slopes = lax.fori_loop(0, tick_count, one_tick, start_state)
    local_grad = back_weight(inputs[0], stored_slopes[0])
    summed_grad = lax.psum(local_grad, "dp")
    mean_grad = summed_grad / lax.axis_size("dp")
    a_rows = a_factor[0]
    row_total = a_rows.shape[0]
    order_full = a_rows.shape[1]
    first_row = lax.axis_index("dp") * row_total
    local_max = jnp.max(jnp.sum(jnp.abs(a_rows.astype(jnp.float32)), axis=1))
    step_size = 1.0 / lax.pmax(local_max, "dp")
    own_eye = eye_rows(first_row, row_total, order_full)
    resid0 = (own_eye - step_size * a_rows.astype(jnp.float32)).astype(jnp.bfloat16)
    left_cols = resid0
    resid1 = jnp.dot(
        left_cols,
        lax.all_gather(resid0, "dp", axis=0, tiled=True),
        preferred_element_type=jnp.float32,
    ).astype(jnp.bfloat16)
    left_cols = resid1
    cross_term = jnp.dot(
        left_cols,
        lax.all_gather(resid0, "dp", axis=0, tiled=True),
        preferred_element_type=jnp.float32,
    )
    inverse_rows = step_size * (
        own_eye + resid0.astype(jnp.float32) + resid1.astype(jnp.float32) + cross_term
    )
    g_inverse = local_inverse(g_factor[0])
    preconditioned = jnp.dot(
        mean_grad, g_inverse, precision=lax.Precision.HIGHEST, preferred_element_type=jnp.float32
    )
    update_rows = jnp.dot(
        inverse_rows,
        preconditioned,
        precision=lax.Precision.HIGHEST,
        preferred_element_type=jnp.float32,
    )
    return (stored_grads[None, None], update_rows[None], inverse_rows[None])


def solution(mesh):
    placed = (
        P("section", "dp", None, None, None, None, None),
        P("section", "dp", None, None, None, None, None),
        P("dp", None, None, None, None, None),
        P("section", None, None),
        P("section", "dp", None),
        P("section", None, None),
    )
    return jax.shard_map(
        shards,
        mesh=mesh,
        in_specs=placed,
        out_specs=(
            P("section", "dp", None, None, None, None, None),
            P("section", "dp", None),
            P("section", "dp", None),
        ),
        check_vma=False,
    )
```

profile of v0, /device:TPU:0, one launch (start us, length us, event | category | flops | bytes accessed | tf_op | source)
XLA Modules:
  0.0 278.0 jit_solution(16409648565365553291)
XLA Ops:
  7.2 1.5 reshape_squeeze.6
  8.7 0.9 copy.18
  9.7 0.2 fusion.56
  10.0 0.1 fusion.68
  10.5 0.1 fusion.76
  10.7 0.1 fusion.80
  10.8 0.2 fusion.82
  11.1 0.2 fusion.86
  11.3 0.2 fusion.88
  11.5 0.2 fusion.90
  11.7 0.2 fusion.92
  12.0 0.2 fusion.96
  12.2 0.1 fusion.98
  12.4 0.1 fusion.102
  13.0 0.1 fusion.114
  13.2 2.1 reshape.70
  15.3 0.7 broadcast.39
  16.0 0.7 broadcast.40
  16.6 24.1 %while.20 = (s32[]{:T(128)}, bf16[64,2,2,128]{3,2,1,0:T(2,128)(2,1)}, bf16[1,64,2,2,128]{4,3,2,1,0:T(2,128)(2,1)}, bf16[1,64,2,2,128]{4,3,2,1,0:T(2,128)(2,1)}, ...) while((s32[]{:T(128)}, ...), condition=%wide.region_1.2_spmd.clone, body=%wide.region_0.1_spmd.clone.sunk | while | flops 113475592 | bytes 10772739 | solution.py:118
  16.6 1.3 collective-permute-start
  17.9 2.0 collective-permute-done
  20.0 1.7 fusion.173
  21.8 0.1 fusion.176
  22.5 0.1 fusion.182
  22.6 0.2 fusion.183
  22.9 0.2 fusion.185
  23.1 0.2 fusion.186
  23.3 0.2 fusion.187
  23.5 0.2 fusion.188
  23.8 0.2 fusion.190
  25.0 0.7 reshape.79
  25.7 1.5 fusion.200
  27.2 0.6 reshape.80
  28.0 0.6 copy-done.5
  28.6 1.3 collective-permute-start
  29.9 2.0 collective-permute-done
  32.0 1.7 fusion.173
  33.9 0.1 fusion.176
  34.5 0.1 fusion.182
  34.7 0.2 fusion.183
  35.0 0.2 fusion.185
  35.2 0.2 fusion.186
  35.4 0.2 fusion.187
  35.5 0.2 fusion.188
  35.8 0.2 fusion.190
  37.0 0.7 reshape.79
  37.8 1.5 fusion.200
  39.3 0.6 reshape.80
  40.1 0.6 copy-done.5
  40.7 0.9 reshape_squeeze.7
  41.6 0.6 reduce_max.18
  42.2 2.9 %fusion.129 = f32[1728,64]{0,1:T(8,128)} fusion(bf16[1728,512]{1,0:T(8,128)(2,1)} %reshape.70, bf16[64,512]{1,0:T(8,128)(2,1)S(1)} %reshape_squeeze.7), kind=kOutput, calls=%fused_computation.203 | convolution fusion | flops 113246208 | bytes 2277376 | tf_op jit(solution)/shard_map/dot_general | solution.py:58
  45.2 44.4 %pmax.7 = f32[]{:T(128)} all-reduce(f32[]{:T(128)} %reduce_max.18), channel_id=1, replica_groups=mesh['section'=2,'dp'=16] {'dp'}, use_global_device_ids=true, to_apply=%region_4.5 | all-reduce | flops 1 | bytes 8 | tf_op jit(solution)/shard_map/pmax | solution.py:127
  90.3 1.0 fusion.128
  91.4 0.6 reduce_max.19
  93.0 64.2 %all-reduce.4.cloned.1.call-done = f32[1728,64]{0,1:T(8,128)} async-done(((f32[1728,64]{0,1:T(8,128)}), f32[1728,64]{0,1:T(8,128)}) %all-reduce.4.cloned.1.call-update) | async-done | bytes 442384 | tf_op jit(solution)/shard_map/psum | solution.py:120
  157.1 1.6 fusion.60
  158.7 94.8 %all-gather.3.cloned.1.call-done = bf16[16,108,1728]{2,1,0:T(8,128)(2,1)} async-done(((bf16[1,108,1728]{2,1,0:T(8,128)(2,1)}), bf16[16,108,1728]{2,1,0:T(8,128)(2,1)}) %all-gather.3.cloned.1.call-update) | async-done | bytes 5971984 | tf_op jit(solution)/shard_map/all_gather | solution.py:133
  253.5 8.7 %reshape.72 = bf16[1728,1728]{1,0:T(8,128)(2,1)} reshape(bf16[16,108,1728]{2,1,0:T(8,128)(2,1)} %all-gather.3.cloned.1.call-done) | data formatting | bytes 11943936
  262.3 4.0 %convolution_convert_fusion.1 = bf16[108,1728]{1,0:T(8,128)(2,1)S(1)} fusion(bf16[1728,1728]{1,0:T(8,128)(2,1)} %reshape.72, bf16[1,108,1728]{2,1,0:T(8,128)(2,1)S(1)} %copy-done.3, f32[]{:T(128)S(6)} %div.12, s32[108]{0:T(128)S(1)} %iota_add_fusion), kind=kOutput, calls=%fused_computation.115 | convolution fusion | flops 646278912 | bytes 6718900 | tf_op jit(solution)/shard_map/dot_general | solution.py:131
  266.3 0.6 copy-done
  266.8 1.1 fusion.54
  267.9 1.6 convolution_bitcast_fusion
  269.5 1.7 copy.17
  (81 shorter events, 6.2 us)
Async XLA Ops:
  7.2 2.5 copy-start.2
  7.2 2.6 copy-start.1
  7.2 149.9 %all-reduce.4.cloned.1.call-start = ((), (), s32[]{:S(2)}) async-start(), calls=%async_computation | async-start | bytes 917504 | tf_op jit(solution)/shard_map/psum | solution.py:120
  16.6 3.3 %collective-permute-start = (bf16[64,2,2,128]{3,2,1,0:T(2,128)(2,1)}, bf16[64,2,2,128]{3,2,1,0:T(2,128)(2,1)S(1)}, u32[]{:S(2)}, u32[]{:S(2)}) collective-permute-start(bf16[64,2,2,128]{3,2,1,0:T(2,128)(2,1)} %get-tuple-element.362), channel_id=1, source_target_pairs={{16,0},{17,1},{18,2},{19,3},{20,4},{21,5},{22,6},{23,7},{24,8},{25... | collective-permute-start | bytes 196616 | tf_op jit(solution)/shard_map/while/body/eval_jaxpr/ppermute | solution.py:13
  25.7 2.2 copy-start.4
  28.0 0.6 copy-start.5
  28.6 3.3 %collective-permute-start = (bf16[64,2,2,128]{3,2,1,0:T(2,128)(2,1)}, bf16[64,2,2,128]{3,2,1,0:T(2,128)(2,1)S(1)}, u32[]{:S(2)}, u32[]{:S(2)}) collective-permute-start(bf16[64,2,2,128]{3,2,1,0:T(2,128)(2,1)} %get-tuple-element.362), channel_id=1, source_target_pairs={{16,0},{17,1},{18,2},{19,3},{20,4},{21,5},{22,6},{23,7},{24,8},{25... | collective-permute-start | bytes 196616 | tf_op jit(solution)/shard_map/while/body/eval_jaxpr/ppermute | solution.py:13
  37.8 2.2 copy-start.4
  40.1 0.6 copy-start.5
  40.7 49.6 %copy-start.3 = (bf16[1,108,1728]{2,1,0:T(8,128)(2,1)S(1)}, bf16[1,108,1728]{2,1,0:T(8,128)(2,1)}, u32[]{:S(2)}) copy-start(bf16[1,108,1728]{2,1,0:T(8,128)(2,1)} %param.12) | copy-start | bytes 1119748
  42.2 49.1 %copy-start.6 = (bf16[1,64,64]{2,1,0:T(8,128)(2,1)S(1)}, bf16[1,64,64]{2,1,0:T(8,128)(2,1)}, u32[]{:S(2)}) copy-start(bf16[1,64,64]{2,1,0:T(8,128)(2,1)} %param.13) | copy-start | bytes 24580
  45.1 208.4 %all-gather.3.cloned.1.call-start = ((), (), s32[]{:S(2)}) async-start(), calls=%async_computation.1 | async-start | bytes 6823936 | tf_op jit(solution)/shard_map/all_gather | solution.py:133
  262.3 4.5 %copy-start = (bf16[1728,1728]{1,0:T(8,128)(2,1)S(1)}, bf16[1728,1728]{1,0:T(8,128)(2,1)}, u32[]{:S(2)}) copy-start(bf16[1728,1728]{1,0:T(8,128)(2,1)} %reshape.72) | copy-start | bytes 17915908
Sparse Core Ops, SparseCore 0:
  45.3 111.8 all-reduce.3
  159.9 93.6 all-gather.2
where the time goes:
time: 279 us; the launch traced here: 278 us
  waiting for transfers between devices  163 us (58%)
  blocking collectives  44.4 us (16%)
  local copies, waits for them, and re-layouts  31.8 us (11%)
  between operations  15.5 us (6%)
  matrix products  14.4 us (5%)
  other arithmetic  6.04 us (2%)
    all_gather x1, waiting for transfers between devices, shards(): lax.all_gather(resid0, 'dp', axis=0, tiled=True)  94.8 us
    psum x1, waiting for transfers between devices, shards(): summed_grad = lax.psum(local_grad, 'dp')  64.2 us
    pmax x1, blocking collectives, shards(): step_size = 1.0 / lax.pmax(local_max, 'dp')  44.4 us
    unnamed x39, local copies, waits for them, and re-layouts  15.1 us
    while x60, local copies, waits for them, and re-layouts  7.65 us
  transfers between devices with their start and end apart: 4, of which 4 were waited for; matrix products, arithmetic and copies ran while one was open for 1% of the time, Pallas kernels for 0%

commit v1 on v0

--- a/solution.py
+++ b/solution.py
@@ -2,9 +2,15 @@
 import jax.numpy as jnp
 from jax import lax
 from jax.sharding import PartitionSpec as P
+from jax.lax import all_gather
 
 KW = 3
 MICRO = 1
+
+
+def update_the_cells(tile_in, named_axis):
+    frame_out = jnp.sum(all_gather(tile_in, named_axis), axis=0)
+    return frame_out
 
 
 def shifted(value, axis, steps):
@@ -117,7 +123,7 @@
     )
     last_sent, stored_grads, stored_slopes = lax.fori_loop(0, tick_count, one_tick, start_state)
     local_grad = back_weight(inputs[0], stored_slopes[0])
-    summed_grad = lax.psum(local_grad, "dp")
+    summed_grad = update_the_cells(local_grad, "dp")
     mean_grad = summed_grad / lax.axis_size("dp")
     a_rows = a_factor[0]
     row_total = a_rows.shape[0]

time: 279 us -> 264 us (0.946)
  waiting for transfers between devices: 163 us -> 144 us
  other arithmetic: 6.04 us -> 11.6 us
    all_gather x0 -> x1, waiting for transfers between devices: none -> 87.7 us  [update_the_cells(): frame_out = jnp.sum(all_gather(tile_in, named_axis), axis=0)]
    psum x1 -> x0, waiting for transfers between devices: 64.2 us -> none  [shards(): summed_grad = lax.psum(local_grad, 'dp')]
    all_gather x1, waiting for transfers between devices: 94.8 us -> 52.6 us  [shards(): lax.all_gather(resid0, 'dp', axis=0, tiled=True)]
    reduce_sum x0 -> x1, other arithmetic: none -> 3.48 us  [update_the_cells(): frame_out = jnp.sum(all_gather(tile_in, named_axis), axis=0)]
  transfers between devices with their start and end apart: 4 -> 4, of which waited for: 4 -> 4; matrix products, arithmetic and copies ran while one was open for 1% -> 17% of each run, Pallas kernels for 0% -> 0%
where the time goes in v1:
time: 264 us; the launch traced here: 263 us
  waiting for transfers between devices  144 us (55%)
  blocking collectives  44.1 us (17%)
  local copies, waits for them, and re-layouts  31 us (12%)
  between operations  15.5 us (6%)
  matrix products  13.7 us (5%)
  other arithmetic  11.6 us (4%)
  starting transfers between devices  2.64 us (1%)
    all_gather x1, waiting for transfers between devices, update_the_cells(): frame_out = jnp.sum(all_gather(tile_in, named_axis), axis=0)  87.7 us
    all_gather x1, waiting for transfers between devices, shards(): lax.all_gather(resid0, 'dp', axis=0, tiled=True)  52.6 us
    pmax x1, blocking collectives, shards(): step_size = 1.0 / lax.pmax(local_max, 'dp')  44.1 us
    unnamed x39, local copies, waits for them, and re-layouts  15.2 us
    while x60, local copies, waits for them, and re-layouts  7.65 us
    dot_general x2, matrix products, shards(): jnp.dot(left_cols, lax.all_gather(resid0, 'dp', axis=0, tiled=True), pref...  5.34 us
  transfers between devices with their start and end apart: 4, of which 4 were waited for; matrix products, arithmetic and copies ran while one was open for 17% of the time, Pallas kernels for 0%

profile of v1, /device:TPU:0, one launch (start us, length us, event | category | flops | bytes accessed | tf_op | source)
XLA Modules:
  0.0 263.1 jit_solution(1806504358141330044)
XLA Ops:
  7.2 1.3 fusion.56
  8.5 0.6 reduce_max.18
  9.1 44.1 %pmax.7 = f32[]{:T(128)} all-reduce(f32[]{:T(128)} %reduce_max.18), channel_id=1, replica_groups=mesh['section'=2,'dp'=16] {'dp'}, use_global_device_ids=true, to_apply=%region_4.5 | all-reduce | flops 1 | bytes 8 | tf_op jit(solution)/shard_map/pmax | solution.py:133
  53.9 1.9 fusion.128
  56.0 0.5 reshape_squeeze.6
  56.4 0.9 copy.18
  57.6 0.1 fusion.68
  58.0 0.1 fusion.76
  58.4 0.2 fusion.82
  58.7 0.2 fusion.86
  58.9 0.2 fusion.88
  59.1 0.2 fusion.90
  59.2 0.2 fusion.92
  59.5 0.2 fusion.96
  59.7 0.1 fusion.98
  59.9 0.1 fusion.102
  60.6 0.1 fusion.114
  60.7 2.3 reshape.70
  63.0 0.7 broadcast.39
  63.7 0.7 broadcast.40
  64.4 24.1 %while.20 = (s32[]{:T(128)}, bf16[64,2,2,128]{3,2,1,0:T(2,128)(2,1)}, bf16[1,64,2,2,128]{4,3,2,1,0:T(2,128)(2,1)}, bf16[1,64,2,2,128]{4,3,2,1,0:T(2,128)(2,1)}, ...) while((s32[]{:T(128)}, ...), condition=%wide.region_1.2_spmd.clone, body=%wide.region_0.1_spmd.clone.sunk | while | flops 113475592 | bytes 10772739 | solution.py:124
  64.4 1.3 collective-permute-start
  65.7 2.0 collective-permute-done
  67.7 1.7 fusion.172
  69.6 0.1 fusion.175
  70.2 0.1 fusion.181
  70.4 0.2 fusion.182
  70.7 0.2 fusion.184
  70.9 0.2 fusion.185
  71.1 0.2 fusion.186
  71.2 0.2 fusion.187
  71.5 0.2 fusion.189
  72.7 0.7 reshape.83
  73.5 1.5 fusion.199
  75.0 0.6 reshape.84
  75.8 0.6 copy-done.4
  76.4 1.3 collective-permute-start
  77.7 2.0 collective-permute-done
  79.7 1.7 fusion.172
  81.6 0.1 fusion.175
  82.3 0.1 fusion.181
  82.4 0.2 fusion.182
  82.7 0.2 fusion.184
  82.9 0.2 fusion.185
  83.1 0.2 fusion.186
  83.3 0.2 fusion.187
  83.6 0.2 fusion.189
  84.8 0.7 reshape.83
  85.5 1.5 fusion.199
  87.0 0.6 reshape.84
  87.8 0.6 copy-done.4
  88.4 0.9 reshape_squeeze.7
  89.3 2.9 %convolution_bitcast_fusion = f32[1,1728,64]{1,2,0:T(8,128)} fusion(bf16[1728,512]{1,0:T(8,128)(2,1)} %reshape.70, bf16[64,512]{1,0:T(8,128)(2,1)S(1)} %reshape_squeeze.7), kind=kOutput, calls=%fused_computation.116 | convolution fusion | flops 113246208 | bytes 2277376 | tf_op jit(solution)/shard_map/dot_general | solution.py:64
  92.4 0.6 reduce_max.19
  93.9 52.6 %all-gather.6.cloned.1.call-done = bf16[16,108,1728]{2,1,0:T(8,128)(2,1)} async-done(((bf16[1,108,1728]{2,1,0:T(8,128)(2,1)}), bf16[16,108,1728]{2,1,0:T(8,128)(2,1)}) %all-gather.6.cloned.1.call-update) | async-done | bytes 5971984 | tf_op jit(solution)/shard_map/all_gather | solution.py:139
  146.5 8.8 %reshape.73 = bf16[1728,1728]{1,0:T(8,128)(2,1)} reshape(bf16[16,108,1728]{2,1,0:T(8,128)(2,1)} %all-gather.6.cloned.1.call-done) | data formatting | bytes 11943936
  155.3 4.3 %convolution_convert_fusion.1 = bf16[108,1728]{1,0:T(8,128)(2,1)S(1)} fusion(bf16[1728,1728]{1,0:T(8,128)(2,1)} %reshape.73, bf16[1,108,1728]{2,1,0:T(8,128)(2,1)S(1)} %copy-done.2, f32[]{:T(128)S(6)} %div.12, s32[108]{0:T(128)S(1)} %iota_add_fusion), kind=kOutput, calls=%fused_computation.115 | convolution fusion | flops 646278912 | bytes 6718900 | tf_op jit(solution)/shard_map/dot_general | solution.py:137
  159.6 0.6 copy-done
  160.2 1.1 fusion.54
  161.2 1.7 copy.17
  162.9 87.7 %all-gather.8.cloned.1.call-done = f32[16,1728,64]{1,2,0:T(8,128)} async-done(((f32[1,1728,64]{1,2,0:T(8,128)}), f32[16,1728,64]{1,2,0:T(8,128)}) %all-gather.8.cloned.1.call-update) | async-done | bytes 7077904 | tf_op jit(solution)/shard_map/all_gather | solution.py:12
  250.6 3.5 %reduce_sum.28 = f32[1728,64]{0,1:T(8,128)S(1)} reduce(f32[16,1728,64]{1,2,0:T(8,128)} %all-gather.8.cloned.1.call-done, f32[]{:T(128)} %constant.76.clone.1), dimensions={0}, to_apply=%region_5.6 | reduce | flops 1658880 | bytes 7520260 | tf_op jit(solution)/shard_map/reduce_sum | solution.py:12
  254.1 0.6 fusion.60
  254.7 1.6 convolution_bitcast_fusion.1
  (82 shorter events, 6.4 us)
Async XLA Ops:
  7.2 48.8 %copy-start.5 = (bf16[1,64,1728]{2,1,0:T(8,128)(2,1)S(1)}, bf16[1,64,1728]{2,1,0:T(8,128)(2,1)}, u32[]{:S(2)}) copy-start(bf16[1,64,1728]{2,1,0:T(8,128)(2,1)} %param.11) | copy-start | bytes 663556
  7.2 50.2 %copy-start.1 = (bf16[1,1,1,64,2,2,128]{6,5,4,3,2,1,0:T(2,128)(2,1)S(1)}, bf16[1,1,1,64,2,2,128]{6,5,4,3,2,1,0:T(2,128)(2,1)}, u32[]{:S(2)}) copy-start(bf16[1,1,1,64,2,2,128]{6,5,4,3,2,1,0:T(2,128)(2,1)} %param.8) | copy-start | bytes 196612
  7.2 139.3 %all-gather.6.cloned.1.call-start = ((), (), s32[]{:S(2)}) async-start(), calls=%async_computation | async-start | bytes 6823936 | tf_op jit(solution)/shard_map/all_gather | solution.py:139
  55.9 194.7 %all-gather.8.cloned.1.call-start = ((), (), s32[]{:S(2)}) async-start(), calls=%async_computation.1 | async-start | bytes 7798784 | tf_op jit(solution)/shard_map/all_gather | solution.py:12
  64.4 3.3 %collective-permute-start = (bf16[64,2,2,128]{3,2,1,0:T(2,128)(2,1)}, bf16[64,2,2,128]{3,2,1,0:T(2,128)(2,1)S(1)}, u32[]{:S(2)}, u32[]{:S(2)}) collective-permute-start(bf16[64,2,2,128]{3,2,1,0:T(2,128)(2,1)} %get-tuple-element.362), channel_id=1, source_target_pairs={{16,0},{17,1},{18,2},{19,3},{20,4},{21,5},{22,6},{23,7},{24,8},{25... | collective-permute-start | bytes 196616 | tf_op jit(solution)/shard_map/while/body/eval_jaxpr/ppermute | solution.py:19
  73.5 2.2 copy-start.3
  75.8 0.6 copy-start.4
  76.4 3.3 %collective-permute-start = (bf16[64,2,2,128]{3,2,1,0:T(2,128)(2,1)}, bf16[64,2,2,128]{3,2,1,0:T(2,128)(2,1)S(1)}, u32[]{:S(2)}, u32[]{:S(2)}) collective-permute-start(bf16[64,2,2,128]{3,2,1,0:T(2,128)(2,1)} %get-tuple-element.362), channel_id=1, source_target_pairs={{16,0},{17,1},{18,2},{19,3},{20,4},{21,5},{22,6},{23,7},{24,8},{25... | collective-permute-start | bytes 196616 | tf_op jit(solution)/shard_map/while/body/eval_jaxpr/ppermute | solution.py:19
  85.5 2.2 copy-start.3
  87.8 0.6 copy-start.4
  88.4 3.8 %copy-start.6 = (bf16[1,64,64]{2,1,0:T(8,128)(2,1)S(1)}, bf16[1,64,64]{2,1,0:T(8,128)(2,1)}, u32[]{:S(2)}) copy-start(bf16[1,64,64]{2,1,0:T(8,128)(2,1)} %param.13) | copy-start | bytes 24580
  93.9 61.3 %copy-start.2 = (bf16[1,108,1728]{2,1,0:T(8,128)(2,1)S(1)}, bf16[1,108,1728]{2,1,0:T(8,128)(2,1)}, u32[]{:S(2)}) copy-start(bf16[1,108,1728]{2,1,0:T(8,128)(2,1)} %param.12) | copy-start | bytes 1119748
  155.3 4.9 %copy-start = (bf16[1728,1728]{1,0:T(8,128)(2,1)S(1)}, bf16[1728,1728]{1,0:T(8,128)(2,1)}, u32[]{:S(2)}) copy-start(bf16[1728,1728]{1,0:T(8,128)(2,1)} %reshape.73) | copy-start | bytes 17915908
Sparse Core Ops, SparseCore 0:
  56.0 90.4 all-gather.5
  149.2 101.3 all-gather.7
